TPU v7x, 32 devices: a whole 2x2x4 slice. The times are simulated.
32 devices in a mesh: groups: 2 (over y), cols: 4 (over z), slab: 2 (over x), rep: 2 (over core).
Axes of the slice: x: 2, y: 2, z: 4, core: 2. Of those that a mesh axis runs over, the one named last changes fastest.
Arguments:
- fields: bfloat16 [16, 8, 2048, 512], P('cols', 'groups', 'rep', 'slab'), parts along dimension 1, may hold values from -250 to 250
- stresses: bfloat16 [6, 8, 512, 128], P(None, 'groups', 'rep', 'slab'), parts along dimension 1, may hold values from -750 to 750
- planes: int32 [8], P('groups'), parts along dimension 0, may hold values from 0 to 2047, as said below
- active_masks: int32 [3, 6, 256], replicated, may hold values 0 or 1
Outputs:
- coefficients: float32 [3, 12, 256], P(None, 'groups', 'cols'), parts along dimension 1
- misfit: bfloat16 [6, 8, 512, 128], P(None, 'groups', 'rep', 'slab'), parts along dimension 1
There are 2 independent parts, one for each index of `groups`. A program takes and returns all parts, laid end to end along the dimension named above; an argument that names none is the same for every part. Nothing has to cross between parts.
Inputs may be any that keep to these rules, and one draw needn't show every extreme that they name: `planes`: sorted and distinct; either the first is 0 or the last is 2047.
All inputs are finite; a program needn't handle non-finite values.
Results may differ from a plain program's by a relative error of at most 0.0069.
Values may be sent and summed in bfloat16 or wider, within the bound.
No kernel may reach another device: no remote copies, remote signals or barrier semaphores. Data moves between devices by JAX's collectives and lax.ppermute only.
A program may use at most 128 MiB of HBM per device.

v0:
```python
import math
import jax
import jax.numpy as jnp
import numpy as np
from jax import lax
from jax.sharding import PartitionSpec as P

STRESS = 6
TERMS = 256
NY = 2048
PASSES = 3
ITERS = 3
ridge_weight = 0.05
epsilon = 1e-06


def extended(array, sides, width):
    for axis, dim in sides:
        count, length = (lax.axis_size(axis), array.shape[dim])
        up = [(i, (i + 1) % count) for i in range(count)]
        down = [(j, i) for i, j in up]
        last = lax.slice_in_dim(array, length - width, length, axis=dim)
        leading = lax.slice_in_dim(array, 0, width, axis=dim)
        before = lax.ppermute(last, axis, up)
        after = lax.ppermute(leading, axis, down)
        array = jnp.concatenate([before, array, after], axis=dim)
    return array


def tree_sum(value, axes):
    for axis in axes:
        count = lax.axis_size(axis)
        if count & count - 1:
            value = lax.psum(value, axis)
            continue
        step = 1
        while step < count:
            partner = [(i, i ^ step) for i in range(count)]
            value = value + lax.ppermute(value, axis, partner)
            step *= 2
    return value


def kernel(spread):
    offsets = np.arange(13) - 6.0
    values = np.exp(-offsets * offsets / (2.0 * spread * spread))
    return values / values.sum()


def filter_table(cells, first_taps, second_taps, guard, order):
    out_count = cells // 4
    shape = tuple(((cells + 10, 2, out_count)[d] for d in order))
    where = {d: order.index(d) for d in range(3)}
    position = lax.broadcasted_iota(jnp.int32, shape, where[0])
    which = lax.broadcasted_iota(jnp.int32, shape, where[1])
    out_index = lax.broadcasted_iota(jnp.int32, shape, where[2])
    tap_at = position - 1 - 4 * out_index + guard
    table = jnp.zeros(shape, jnp.float32)
    for tap_index in range(13):
        value = jnp.where(
            which == 0, np.float32(first_taps[tap_index]), np.float32(second_taps[tap_index])
        )
        table = jnp.where(tap_at == tap_index, value, table)
    return table


def library(narrow_part, broad_part):
    product = (
        narrow_part.astype(jnp.float32)[:, None, :] * broad_part.astype(jnp.float32)[None, :, :]
    )
    return product.astype(jnp.bfloat16).reshape(
        narrow_part.shape[0] * broad_part.shape[0], narrow_part.shape[1]
    )


def local(fields, stresses, planes, active_masks):
    chan_dev, plane_count, cells_x, cells_z = fields.shape
    coarse_x = cells_x // 4
    coarse_z = cells_z // 4
    row_count = plane_count * coarse_x * coarse_z
    col_devices = lax.axis_size("cols")
    column_index = lax.axis_index("cols")
    term_dev = TERMS // col_devices
    offset = column_index * term_dev
    samples = float(row_count * lax.axis_size("slab") * lax.axis_size("rep"))
    height = 2.0 * (planes.astype(jnp.float32) + 0.5) / NY - 1.0
    root_weight = jnp.sqrt(1.2 - height * height)
    padded = extended(fields, (("slab", 3), ("rep", 2)), 5)
    widened = padded.astype(jnp.float32)
    narrow_taps = kernel(1.5)
    broad_taps = kernel(3.0)
    guard = jnp.minimum(lax.axis_index("rep"), 0)
    span_table = filter_table(cells_z, narrow_taps, broad_taps, guard, (0, 1, 2))
    stream_table = filter_table(cells_x, narrow_taps, broad_taps, guard, (1, 0, 2))
    along_span = jnp.einsum("cpxz,zsn->cpxsn", widened, span_table, precision=lax.Precision.HIGHEST)
    filtered = jnp.einsum(
        "cpxsn,sxm->scpmn", along_span, stream_table, precision=lax.Precision.HIGHEST
    )
    narrow = filtered[0]
    broader = filtered[1]
    narrow_set = narrow.astype(jnp.bfloat16).reshape(chan_dev, row_count)
    broad_set = (
        (broader * root_weight[None, :, None, None])
        .astype(jnp.bfloat16)
        .reshape(chan_dev, row_count)
    )
    weighted = (stresses.astype(jnp.float32) * root_weight[None, :, None, None]).astype(
        jnp.bfloat16
    )
    weighted = weighted.reshape(STRESS, row_count)
    chunk = row_count // col_devices
    block_rows = math.gcd(chunk, 4096)
    block_count = chunk // block_rows
    both_sets = lax.all_to_all(jnp.stack([narrow_set, broad_set]), "cols", 2, 1, tiled=True)
    narrow_all, broad_all = (both_sets[0], both_sets[1])
    weighted = lax.dynamic_slice_in_dim(weighted, column_index * chunk, chunk, 1)

    def gram_step(block_index, carry):
        gram_acc, rhs_acc = carry
        start = block_index * block_rows
        narrow_piece = lax.dynamic_slice_in_dim(narrow_all, start, block_rows, 1)
        broad_piece = lax.dynamic_slice_in_dim(broad_all, start, block_rows, 1)
        all_terms = library(narrow_piece, broad_piece)
        weighted_piece = lax.dynamic_slice_in_dim(weighted, start, block_rows, 1)
        gram_acc = gram_acc + jnp.einsum(
            "ir,jr->ij", all_terms, all_terms, preferred_element_type=jnp.float32
        )
        rhs_acc = rhs_acc + jnp.einsum(
            "ir,kr->ik", all_terms, weighted_piece, preferred_element_type=jnp.float32
        )
        return (gram_acc, rhs_acc)

    gram_part, rhs_part = lax.fori_loop(
        0,
        block_count,
        gram_step,
        (jnp.zeros((TERMS, TERMS), jnp.float32), jnp.zeros((TERMS, STRESS), jnp.float32)),
    )
    full_rows = tree_sum(jnp.concatenate([gram_part, rhs_part], axis=1), ("rep", "slab", "cols"))
    gram_matrix = full_rows[:, :TERMS]
    rhs_sums = full_rows[:, TERMS:]
    column_scale = 1.0 / jnp.sqrt(jnp.diagonal(gram_matrix) / samples + epsilon)
    normal_gram = column_scale[:, None] * gram_matrix * column_scale[None, :] / samples
    target_norm = column_scale[None, :] * rhs_sums.T / samples

    def apply_normal(vector, active):
        product = jnp.einsum(
            "kl,il->ki", active * vector, normal_gram, precision=lax.Precision.HIGHEST
        )
        return active * product + ridge_weight * vector

    def cg_turn(turn_index, state):
        solution_all, remain, direction, norm_now, active = state
        applied = apply_normal(direction, active)
        curve_sum = jnp.sum(direction * applied, axis=1)
        step_size = norm_now / (curve_sum + epsilon)
        solution_all = solution_all + step_size[:, None] * direction
        remain = remain - step_size[:, None] * applied
        norm_next = jnp.sum(remain * remain, axis=1)
        direction = remain + (norm_next / (norm_now + epsilon))[:, None] * direction
        return (solution_all, remain, direction, norm_next, active)

    def cg_pass(pass_index, state):
        solution_all, coefficients = state
        active = lax.dynamic_index_in_dim(active_masks, pass_index, 0, keepdims=False)
        active = active.astype(jnp.float32)
        solution_all = active * solution_all
        remain = active * target_norm - apply_normal(solution_all, active)
        norm_now = jnp.sum(remain * remain, axis=1)
        solution_all = lax.fori_loop(
            0, ITERS, cg_turn, (solution_all, remain, remain, norm_now, active)
        )[0]
        own_part = lax.dynamic_slice_in_dim(solution_all, offset, term_dev, 1)
        coefficients = lax.dynamic_update_index_in_dim(coefficients, own_part, pass_index, 0)
        return (solution_all, coefficients)

    solution_all, coefficients = lax.fori_loop(
        0,
        PASSES,
        cg_pass,
        (
            jnp.zeros((STRESS, TERMS), jnp.float32),
            jnp.zeros((PASSES, STRESS, term_dev), jnp.float32),
        ),
    )
    final_weights = (column_scale[None, :] * solution_all).astype(jnp.bfloat16)

    def misfit_step(block_index, misfit_acc):
        start = block_index * block_rows
        narrow_piece = lax.dynamic_slice_in_dim(narrow_all, start, block_rows, 1)
        broad_piece = lax.dynamic_slice_in_dim(broad_all, start, block_rows, 1)
        all_terms = library(narrow_piece, broad_piece)
        predicted = jnp.dot(final_weights, all_terms, preferred_element_type=jnp.float32)
        weighted_piece = lax.dynamic_slice_in_dim(weighted, start, block_rows, 1)
        piece_misfit = (weighted_piece.astype(jnp.float32) - predicted).astype(jnp.bfloat16)
        return lax.dynamic_update_slice_in_dim(misfit_acc, piece_misfit, start, 1)

    misfit = lax.fori_loop(0, block_count, misfit_step, jnp.zeros((STRESS, chunk), jnp.bfloat16))
    misfit = lax.all_gather(misfit, "cols", axis=1, tiled=True)
    misfit = misfit.reshape(STRESS, plane_count, coarse_x, coarse_z)
    return (coefficients, misfit)


def solution(mesh):
    placed = (
        P("cols", "groups", "rep", "slab"),
        P(None, "groups", "rep", "slab"),
        P("groups"),
        P(),
    )
    return jax.shard_map(
        local,
        mesh=mesh,
        in_specs=placed,
        out_specs=(P(None, "groups", "cols"), P(None, "groups", "rep", "slab")),
        check_vma=False,
    )
```

profile of v0, /device:TPU:0, one launch (start us, length us, event | category | flops | bytes accessed | tf_op | source)
XLA Modules:
  0.0 642.4 jit_solution(13972069590268491912)
XLA Ops:
  0.7 11.6 %copy.29 = bf16[4,4,1024,256]{2,3,1,0:T(8,128)(2,1)} copy(bf16[4,4,1024,256]{3,2,1,0:T(8,128)(2,1)} %param.12) | data formatting | bytes 16777216 | tf_op args[0]
  13.4 3.0 collective-permute-start
  16.9 6.6 %collective-permute-done = bf16[4,4,1024,5]{2,3,1,0:T(8,128)(2,1)S(1)} collective-permute-done((bf16[4,4,1024,5]{2,3,1,0:T(8,128)(2,1)S(1)}, bf16[4,4,1024,5]{2,3,1,0:T(8,128)(2,1)S(1)}, u32[]{:S(2)}, u32[]{:S(2)}) %collective-permute-start) | collective-permute-done | bytes 163872 | tf_op jit(solution)/shard_map/ppermute | solution.py:24
  23.5 4.8 collective-permute-done.1
  28.3 5.5 pad_maximum_fusion
  33.8 3.5 copy-done
  45.0 18.4 %concatenate.14 = bf16[4,4,1034,266]{2,3,1,0:T(8,128)(2,1)} concatenate(bf16[4,4,5,266]{2,3,1,0:T(8,128)(2,1)S(1)} %copy.34, bf16[4,4,1024,266]{2,3,1,0:T(8,128)(2,1)} %copy-done, bf16[4,4,5,266]{2,3,1,0:T(8,128)(2,1)S(1)} %copy.35), dimensions={2} | concatenate | bytes 17602816 | tf_op jit(solution)/shard_map/concatenate | solution.py:26
  63.4 10.7 %fusion.10 = f32[4,4,1034,2,64]{2,4,1,0,3:T(8,128)S(1)} fusion(bf16[4,4,1034,266]{2,3,1,0:T(8,128)(2,1)} %concatenate.14, f32[2]{0:T(128)S(1)} %get-tuple-element.567, f32[2]{0:T(128)S(1)} %get-tuple-element.568, f32[2]{0:T(128)S(1)} %get-tuple-element.569, f32[2]{0:T(128)S(1)} %get-tuple-element.570, f32[2]{0:T(128)S(1)} %get-tuple-element.571, ...), kind=kOutput, calls=%fused_computation.32 | convolution fusion | flops 6760434688 | bytes 17273316 | tf_op jit(solution)/shard_map/cpxz,zsn->cpxsn/dot_general | solution.py:95
  74.2 10.1 %fusion.53 = f32[2,4,4,256,64]{3,4,2,1,0:T(8,128)S(1)} fusion(f32[4,4,1034,2,64]{2,4,1,0,3:T(8,128)S(1)} %fusion.10, f32[2]{0:T(128)S(1)} %get-tuple-element.567, f32[2]{0:T(128)S(1)} %get-tuple-element.568, f32[2]{0:T(128)S(1)} %get-tuple-element.569, f32[2]{0:T(128)S(1)} %get-tuple-element.570, f32[2]{0:T(128)S(1)} %get-tuple-element.571, ...), kind=kOutput, calls=%fused_computation.64 | convolution fusion | flops 6520188928 | bytes 10572900 | tf_op jit(solution)/shard_map/cpxsn,sxm->scpmn/dot_general | solution.py:96
  90.9 50.9 %copy.38 = bf16[2,4,65536]{1,0,2:T(2,128)(2,1)} copy(bf16[2,4,65536]{2,1,0:T(4,128)(2,1)S(1)} %pad_maximum_fusion.1) | data formatting | bytes 2097152 | tf_op jit(solution)/shard_map/stack | solution.py:114
  141.8 99.7 %reshape.126 = bf16[4,2,65536]{2,1,0:T(2,128)(2,1)} reshape(bf16[65536,2,4]{2,1,0:T(2,128)(2,1)} %bitcast.80) | data formatting | bytes 2097152
  241.5 5.1 all-to-all-start
  248.3 24.3 %all-to-all-done = bf16[4,2,65536]{2,1,0:T(2,128)(2,1)S(1)} async-done(((bf16[4,2,65536]{2,1,0:T(2,128)(2,1)}), bf16[4,2,65536]{2,1,0:T(2,128)(2,1)S(1)}, u32[]{:S(2)}, u32[]{:S(2)}) %all-to-all-start) | async-done | bytes 1048608 | tf_op jit(solution)/shard_map/all_to_all | solution.py:114
  272.6 85.1 %reshape.127 = bf16[65536,2,4]{2,1,0:T(2,128)(2,1)} reshape(bf16[4,2,65536]{2,1,0:T(2,128)(2,1)S(1)} %all-to-all-done) | data formatting | bytes 2097152
  357.7 62.4 %fusion.183 = (bf16[1,4,4,16384]{2,0,3,1:T(2,128)(2,1)}, bf16[1,4,4,16384]{2,0,3,1:T(2,128)(2,1)}) fusion(bf16[2,4,4,16384]{2,0,3,1:T(2,128)(2,1)} %bitcast.78), kind=kLoop, calls=%fused_computation.197 | loop fusion | bytes 2097152 | tf_op jit(solution)/shard_map/slice | solution.py:115
  420.1 61.1 %copy.39 = bf16[1,4,4,16384]{3,2,1,0:T(4,128)(2,1)S(1)} copy(bf16[1,4,4,16384]{2,0,3,1:T(2,128)(2,1)} %get-tuple-element.562) | data formatting | bytes 1048576 | tf_op jit(solution)/shard_map/slice | solution.py:115
  481.3 61.1 %copy.40 = bf16[1,4,4,16384]{3,2,1,0:T(4,128)(2,1)S(1)} copy(bf16[1,4,4,16384]{2,0,3,1:T(2,128)(2,1)} %get-tuple-element.561) | data formatting | bytes 1048576 | tf_op jit(solution)/shard_map/slice | solution.py:115
  542.5 11.0 %while.79 = (s32[]{:T(128)}, f32[256,256]{1,0:T(8,128)S(1)}, f32[256,6]{0,1:T(8,128)S(1)}, bf16[16,16384]{1,0:T(8,128)(2,1)S(1)}, bf16[16,16384]{1,0:T(8,128)(2,...) while((s32[]{:T(128)}, f32[256,256]{1,0:T(8,128)S(1)}, ...), condition=%wide.region_1.2_spmd.clone, body=%wide.region_0.1_spmd.clone.sunk | while | flops 551816192 | bytes 8204454 | solution.py:133
  557.1 9.7 %collective-permute-done.5 = f32[256,262]{1,0:T(8,128)S(1)} collective-permute-done((f32[256,262]{1,0:T(8,128)S(1)}, f32[256,262]{1,0:T(8,128)S(1)}, u32[]{:S(2)}, u32[]{:S(2)}) %collective-permute-start.5) | collective-permute-done | bytes 268320 | tf_op jit(solution)/shard_map/ppermute | solution.py:39
  566.9 10.3 %collective-permute-done.6 = f32[256,262]{1,0:T(8,128)S(1)} collective-permute-done((f32[256,262]{1,0:T(8,128)S(1)}, f32[256,262]{1,0:T(8,128)S(1)}, u32[]{:S(2)}, u32[]{:S(2)}) %collective-permute-start.6) | collective-permute-done | bytes 268320 | tf_op jit(solution)/shard_map/ppermute | solution.py:39
  577.6 18.5 %collective-permute-done.7 = f32[256,262]{1,0:T(8,128)S(1)} collective-permute-done((f32[256,262]{1,0:T(8,128)S(1)}, f32[256,262]{1,0:T(8,128)S(1)}, u32[]{:S(2)}, u32[]{:S(2)}) %collective-permute-start.7) | collective-permute-done | bytes 268320 | tf_op jit(solution)/shard_map/ppermute | solution.py:39
  598.8 12.1 %while.77 = (s32[]{:T(128)}, f32[6,256]{1,0:T(8,128)S(1)}, f32[3,6,64]{2,1,0:T(8,128)}, s32[3,6,256]{2,1,0:T(8,128)}, f32[6,256]{1,0:T(8,128)S(1)}, /*index=5*/f...) while((s32[]{:T(128)}, f32[6,256]{1,0:T(8,128)S(1)}, f32[3,6,64]{2,1,0:T(8,128)}, ...), condition=%wide.region_8.9_spmd, body=%wide.region_2.8_spmd.sunk | while | flops 9474058 | bytes 660566 | solution.py:177
  610.9 6.4 %while.78 = (s32[]{:T(128)}, bf16[6,16384]{1,0:T(8,128)(2,1)S(1)}, bf16[6,16384]{1,0:T(8,128)(2,1)}, bf16[16,16384]{1,0:T(8,128)(2,1)S(1)}, bf16[16,16384]{1,0:T...) while((s32[]{:T(128)}, bf16[6,16384]{1,0:T(8,128)(2,1)S(1)}, ...), condition=%wide.region_10.11_spmd, body=%wide.region_9.10_spmd.sunk | while | flops 14884870 | bytes 5623963 | solution.py:198
  617.4 21.5 %all_gather.3 = bf16[6,65536]{1,0:T(8,128)(2,1)S(1)} all-gather(bf16[6,16384]{1,0:T(8,128)(2,1)S(1)} %get-tuple-element.439), channel_id=1, replica_groups=mesh['groups'=2,'cols'=4,'slab'=2,'rep'=2] {'cols'}, dimensions={1}, use_global_device_ids=true | all-gather | bytes 983040 | tf_op jit(solution)/shard_map/all_gather | solution.py:199
  (164 shorter events, 63.1 us)
Async XLA Ops:
  0.6 15.8 %copy-start.2 = (s32[4]{0:T(128)S(1)}, s32[4]{0:T(128)}, u32[]{:S(2)}) copy-start(s32[4]{0:T(128)} %param.14) | copy-start | bytes 52
  0.6 15.9 %copy-start.1 = (bf16[6,4,256,64]{2,3,1,0:T(8,128)(2,1)S(1)}, bf16[6,4,256,64]{2,3,1,0:T(8,128)(2,1)}, u32[]{:S(2)}) copy-start(bf16[6,4,256,64]{2,3,1,0:T(8,128)(2,1)} %param.13) | copy-start | bytes 2359300
  13.4 10.1 %collective-permute-start = (bf16[4,4,1024,5]{2,3,1,0:T(8,128)(2,1)S(1)}, bf16[4,4,1024,5]{2,3,1,0:T(8,128)(2,1)S(1)}, u32[]{:S(2)}, u32[]{:S(2)}) collective-permute-start(bf16[4,4,1024,5]{2,3,1,0:T(8,128)(2,1)S(1)} %get-tuple-element.565), channel_id=1, source_target_pairs={{0,2},{2,0},{1,3},{3,1},{4,6},{6,4},{5,7},{7,5},{8,10},{10,8},{9,1... | collective-permute-start | bytes 491528 | tf_op jit(solution)/shard_map/ppermute | solution.py:24
  16.4 11.9 %collective-permute-start.1 = (bf16[4,4,1024,5]{2,3,1,0:T(8,128)(2,1)S(1)}, bf16[4,4,1024,5]{2,3,1,0:T(8,128)(2,1)S(1)}, u32[]{:S(2)}, u32[]{:S(2)}) collective-permute-start(bf16[4,4,1024,5]{2,3,1,0:T(8,128)(2,1)S(1)} %get-tuple-element.566), channel_id=1, source_target_pairs={{2,0},{0,2},{3,1},{1,3},{6,4},{4,6},{7,5},{5,7},{10,8},{8,10},{11,... | collective-permute-start | bytes 491528 | tf_op jit(solution)/shard_map/ppermute | solution.py:25
  33.8 3.5 copy-start
  38.5 5.3 collective-permute-start.2
  39.1 5.3 collective-permute-start.3
  241.5 31.1 %all-to-all-start = ((bf16[4,2,65536]{2,1,0:T(2,128)(2,1)}), bf16[4,2,65536]{2,1,0:T(2,128)(2,1)S(1)}, u32[]{:S(2)}, u32[]{:S(2)}) async-start(bf16[4,2,65536]{2,1,0:T(2,128)(2,1)} %reshape.126), calls=%async_computation | async-start | bytes 2097152 | tf_op jit(solution)/shard_map/all_to_all | solution.py:114
  553.7 1.8 collective-permute-start.4
  555.5 11.2 %collective-permute-start.5 = (f32[256,262]{1,0:T(8,128)S(1)}, f32[256,262]{1,0:T(8,128)S(1)}, u32[]{:S(2)}, u32[]{:S(2)}) collective-permute-start(f32[256,262]{1,0:T(8,128)S(1)} %fusion.181), channel_id=1, source_target_pairs={{0,2},{2,0},{1,3},{3,1},{4,6},{6,4},{5,7},{7,5},{8,10},{10,8},{9,1... | collective-permute-start | bytes 804872 | tf_op jit(solution)/shard_map/ppermute | solution.py:39
  566.8 10.4 %collective-permute-start.6 = (f32[256,262]{1,0:T(8,128)S(1)}, f32[256,262]{1,0:T(8,128)S(1)}, u32[]{:S(2)}, u32[]{:S(2)}) collective-permute-start(f32[256,262]{1,0:T(8,128)S(1)} %add.190), channel_id=1, source_target_pairs={{0,4},{4,0},{8,12},{12,8},{1,5},{5,1},{9,13},{13,9},{2,6},{6,2},{1... | collective-permute-start | bytes 804872 | tf_op jit(solution)/shard_map/ppermute | solution.py:39
  577.2 18.8 %collective-permute-start.7 = (f32[256,262]{1,0:T(8,128)S(1)}, f32[256,262]{1,0:T(8,128)S(1)}, u32[]{:S(2)}, u32[]{:S(2)}) collective-permute-start(f32[256,262]{1,0:T(8,128)S(1)} %add.191), channel_id=1, source_target_pairs={{0,8},{4,12},{8,0},{12,4},{1,9},{5,13},{9,1},{13,5},{2,10},{6,14},... | collective-permute-start | bytes 804872 | tf_op jit(solution)/shard_map/ppermute | solution.py:39
where the time goes:
time: 654 us; the launch traced here: 642 us
  local copies, waits for them, and re-layouts  476 us (73%)
  waiting for transfers between devices  75.8 us (12%)
  matrix products  40.1 us (6%)
  blocking collectives  21.5 us (3%)
  other arithmetic  15.8 us (2%)
  starting transfers between devices  10.9 us (2%)
    unnamed x10, local copies, waits for them, and re-layouts  201 us
    slice x3, local copies, waits for them, and re-layouts, local(): narrow_all, broad_all = (both_sets[0], both_sets[1])  185 us
    another operation x1, local copies, waits for them, and re-layouts, local(): jnp.stack([narrow_set, broad_set])  50.9 us
    ppermute x4, waiting for transfers between devices, tree_sum(): value = value + lax.ppermute(value, axis, partner)  40.1 us
    all_to_all x1, waiting for transfers between devices, local(): lax.all_to_all(jnp.stack([narrow_set, broad_set]), 'cols', 2, 1, tiled=True)  24.3 us
    all_gather x1, blocking collectives, local(): misfit = lax.all_gather(misfit, 'cols', axis=1, tiled=True)  21.5 us
    concatenate x1, local copies, waits for them, and re-layouts, extended(): array = jnp.concatenate([before, array, after], axis=dim)  18.4 us
  transfers between devices with their start and end apart: 9, of which 7 were waited for; matrix products, arithmetic and copies ran while one was open for 1% of the time, Pallas kernels for 0%

commit v1 on v0

--- a/solution.py
+++ b/solution.py
@@ -111,7 +111,16 @@
     chunk = row_count // col_devices
     block_rows = math.gcd(chunk, 4096)
     block_count = chunk // block_rows
-    both_sets = lax.all_to_all(jnp.stack([narrow_set, broad_set]), "cols", 2, 1, tiled=True)
+    shard = jnp.stack([narrow_set, broad_set])
+    ways, here = (lax.axis_size("cols"), lax.axis_index("cols"))
+    width_2 = shard.shape[2] // ways
+    turned = jnp.roll(shard, -here * width_2, axis=2)
+    got = [lax.slice_in_dim(turned, 0, width_2, axis=2)]
+    for far in range(1, ways):
+        sent = lax.slice_in_dim(turned, far * width_2, (far + 1) * width_2, axis=2)
+        got.append(lax.ppermute(sent, "cols", [(d_2, (d_2 + far) % ways) for d_2 in range(ways)]))
+    line = jnp.concatenate(got[::-1], axis=1)
+    both_sets = jnp.roll(line, (here + 1) * got[0].shape[1], axis=1)
     narrow_all, broad_all = (both_sets[0], both_sets[1])
     weighted = lax.dynamic_slice_in_dim(weighted, column_index * chunk, chunk, 1)
 

time: 654 us -> 222 us (0.34); the launches traced: 642 us -> 220 us
  local copies, waits for them, and re-layouts: 476 us -> 57.3 us
  waiting for transfers between devices: 75.8 us -> 68.1 us
    unnamed x10 -> x8, local copies, waits for them, and re-layouts: 201 us -> 16.5 us
    slice x3 -> x1, local copies, waits for them, and re-layouts: 185 us -> 0.36 us  [local(): got = [lax.slice_in_dim(turned, 0, width_2, axis=2)]]
    another operation x1 -> x0, local copies, waits for them, and re-layouts: 50.9 us -> none  [local(): jnp.stack([narrow_set, broad_set])]
    all_to_all x1 -> x0, waiting for transfers between devices: 24.3 us -> none  [local(): lax.all_to_all(jnp.stack([narrow_set, broad_set]), 'cols', 2, 1, tiled=True)]
    ppermute x0 -> x3, waiting for transfers between devices: none -> 19.8 us  [local(): lax.ppermute(sent, 'cols', [(d_2, (d_2 + far) % ways) for d_2 in range(wa...]
  transfers between devices with their start and end apart: 9 -> 11, of which waited for: 7 -> 8; matrix products, arithmetic and copies ran while one was open for 1% -> 3% of each run, Pallas kernels for 0% -> 0%
where the time goes in v1:
time: 222 us; the launch traced here: 220 us
  waiting for transfers between devices  68.1 us (31%)
  local copies, waits for them, and re-layouts  57.3 us (26%)
  matrix products  40.1 us (18%)
  blocking collectives  21.9 us (10%)
  other arithmetic  17.4 us (8%)
  starting transfers between devices  14 us (6%)
    ppermute x4, waiting for transfers between devices, tree_sum(): value = value + lax.ppermute(value, axis, partner)  36.9 us
    all_gather x1, blocking collectives, local(): misfit = lax.all_gather(misfit, 'cols', axis=1, tiled=True)  21.9 us
    ppermute x3, waiting for transfers between devices, local(): lax.ppermute(sent, 'cols', [(d_2, (d_2 + far) % ways) for d_2 in range(wa...  19.8 us
    concatenate x1, local copies, waits for them, and re-layouts, extended(): array = jnp.concatenate([before, array, after], axis=dim)  18.4 us
    unnamed x8, local copies, waits for them, and re-layouts  16.5 us
    dot_general x1, matrix products, local(): jnp.einsum('cpxz,zsn->cpxsn', widened, span_table, precision=lax.Precisio...  10.7 us
    dot_general x1, matrix products, local(): jnp.einsum('cpxsn,sxm->scpmn', along_span, stream_table, precision=lax.Pr...  10.1 us
    ppermute x2, waiting for transfers between devices, extended(): before = lax.ppermute(last, axis, up)  6.6 us
  transfers between devices with their start and end apart: 11, of which 8 were waited for; matrix products, arithmetic and copies ran while one was open for 3% of the time, Pallas kernels for 0%

profile of v1, /device:TPU:0, one launch (start us, length us, event | category | flops | bytes accessed | tf_op | source)
XLA Modules:
  0.0 220.2 jit_solution(13930438757617862853)
XLA Ops:
  0.7 11.6 %copy.24 = bf16[4,4,1024,256]{2,3,1,0:T(8,128)(2,1)} copy(bf16[4,4,1024,256]{3,2,1,0:T(8,128)(2,1)} %param.12) | data formatting | bytes 16777216 | tf_op args[0]
  13.4 3.0 %collective-permute-start = (bf16[4,4,1024,5]{2,3,1,0:T(8,128)(2,1)S(1)}, bf16[4,4,1024,5]{2,3,1,0:T(8,128)(2,1)S(1)}, u32[]{:S(2)}, u32[]{:S(2)}) collective-permute-start(bf16[4,4,1024,5]{2,3,1,0:T(8,128)(2,1)S(1)} %get-tuple-element.563), channel_id=1, source_target_pairs={{0,2},{2,0},{1,3},{3,1},{4,6},{6,4},{5,7},{7,5},{8,10},{10,8},{9,1... | collective-permute-start | bytes 491528 | tf_op jit(solution)/shard_map/ppermute | solution.py:24
  16.9 6.6 %collective-permute-done = bf16[4,4,1024,5]{2,3,1,0:T(8,128)(2,1)S(1)} collective-permute-done((bf16[4,4,1024,5]{2,3,1,0:T(8,128)(2,1)S(1)}, bf16[4,4,1024,5]{2,3,1,0:T(8,128)(2,1)S(1)}, u32[]{:S(2)}, u32[]{:S(2)}) %collective-permute-start) | collective-permute-done | bytes 163872 | tf_op jit(solution)/shard_map/ppermute | solution.py:24
  23.5 4.8 %collective-permute-done.1 = bf16[4,4,1024,5]{2,3,1,0:T(8,128)(2,1)S(1)} collective-permute-done((bf16[4,4,1024,5]{2,3,1,0:T(8,128)(2,1)S(1)}, bf16[4,4,1024,5]{2,3,1,0:T(8,128)(2,1)S(1)}, u32[]{:S(2)}, u32[]{:S(2)}) %collective-permute-start.1) | collective-permute-done | bytes 163872 | tf_op jit(solution)/shard_map/ppermute | solution.py:25
  28.3 5.5 %pad_maximum_fusion = bf16[4,4,1024,266]{2,3,1,0:T(8,128)(2,1)S(1)} fusion(bf16[4,4,1024,5]{2,3,1,0:T(8,128)(2,1)S(1)} %collective-permute-done.1, bf16[4,4,1024,256]{2,3,1,0:T(8,128)(2,1)} %copy.24, bf16[4,4,1024,5]{2,3,1,0:T(8,128)(2,1)S(1)} %collective-permute-done), kind=kLoop, calls=%fused_computation.34 | loop fusion | flops 26148864 | bytes 17432576 | tf_op jit(solution)/shard_map/concatenate | solution.py:26
  33.8 3.5 %copy-done = bf16[4,4,1024,266]{2,3,1,0:T(8,128)(2,1)} copy-done((bf16[4,4,1024,266]{2,3,1,0:T(8,128)(2,1)}, bf16[4,4,1024,266]{2,3,1,0:T(8,128)(2,1)S(1)}, u32[]{:S(2)}) %copy-start) | copy-done | bytes 8716312
  40.8 2.3 %reshape.111 = bf16[6,65536]{1,0:T(8,128)(2,1)} reshape(bf16[6,4,256,64]{3,2,1,0:T(8,128)(2,1)S(1)} %copy.33) | data formatting | bytes 1572864 | tf_op jit(solution)/shard_map/reshape | solution.py:110
  44.3 18.4 %concatenate.24 = bf16[4,4,1034,266]{2,3,1,0:T(8,128)(2,1)} concatenate(bf16[4,4,5,266]{2,3,1,0:T(8,128)(2,1)S(1)} %copy.29, bf16[4,4,1024,266]{2,3,1,0:T(8,128)(2,1)} %copy-done, bf16[4,4,5,266]{2,3,1,0:T(8,128)(2,1)S(1)} %copy.30), dimensions={2} | concatenate | bytes 17602816 | tf_op jit(solution)/shard_map/concatenate | solution.py:26
  62.7 10.7 %fusion.10 = f32[4,4,1034,2,64]{2,4,1,0,3:T(8,128)S(1)} fusion(bf16[4,4,1034,266]{2,3,1,0:T(8,128)(2,1)} %concatenate.24, f32[2]{0:T(128)S(1)} %get-tuple-element.571, f32[2]{0:T(128)S(1)} %get-tuple-element.572, f32[2]{0:T(128)S(1)} %get-tuple-element.573, f32[2]{0:T(128)S(1)} %get-tuple-element.574, f32[2]{0:T(128)S(1)} %get-tuple-element.575, ...), kind=kOutput, calls=%fused_computation.32 | convolution fusion | flops 6760434688 | bytes 17273316 | tf_op jit(solution)/shard_map/cpxz,zsn->cpxsn/dot_general | solution.py:95
  73.4 10.1 %fusion.53 = f32[2,4,4,256,64]{3,4,2,1,0:T(8,128)S(1)} fusion(f32[4,4,1034,2,64]{2,4,1,0,3:T(8,128)S(1)} %fusion.10, f32[2]{0:T(128)S(1)} %get-tuple-element.571, f32[2]{0:T(128)S(1)} %get-tuple-element.572, f32[2]{0:T(128)S(1)} %get-tuple-element.573, f32[2]{0:T(128)S(1)} %get-tuple-element.574, f32[2]{0:T(128)S(1)} %get-tuple-element.575, ...), kind=kOutput, calls=%fused_computation.68 | convolution fusion | flops 6520188928 | bytes 10572900 | tf_op jit(solution)/shard_map/cpxsn,sxm->scpmn/dot_general | solution.py:96
  88.4 3.3 %fusion.81 = bf16[2,4,65536]{2,1,0:T(4,128)(2,1)S(1)} fusion(s32[]{:T(128)S(6)} %select_n.276, bf16[1,4,65536]{2,1,0:T(4,128)(2,1)S(1)} %convert_element_type.125, bf16[1,4,65536]{2,1,0:T(4,128)(2,1)S(1)} %multiply_convert_fusion.3), kind=kLoop, calls=%fused_computation.95 | loop fusion | flops 4194304 | bytes 2097156 | tf_op jit(solution)/shard_map/jit(_roll_dynamic)/concatenate | solution.py:117
  92.2 3.9 %collective-permute-start.4 = (bf16[2,4,16384]{2,1,0:T(4,128)(2,1)S(1)}, bf16[2,4,16384]{2,1,0:T(4,128)(2,1)S(1)}, u32[]{:S(2)}, u32[]{:S(2)}) collective-permute-start(bf16[2,4,16384]{2,1,0:T(4,128)(2,1)S(1)} %get-tuple-element.570), channel_id=1, source_target_pairs={{0,12},{4,0},{8,4},{12,8},{1,13},{5,1},{9,5},{13,9},{2,14},{6,2},{... | collective-permute-start | bytes 786440 | tf_op jit(solution)/shard_map/ppermute | solution.py:121
  98.7 4.1 %collective-permute-done.4 = bf16[2,4,16384]{2,1,0:T(4,128)(2,1)S(1)} collective-permute-done((bf16[2,4,16384]{2,1,0:T(4,128)(2,1)S(1)}, bf16[2,4,16384]{2,1,0:T(4,128)(2,1)S(1)}, u32[]{:S(2)}, u32[]{:S(2)}) %collective-permute-start.4) | collective-permute-done | bytes 262176 | tf_op jit(solution)/shard_map/ppermute | solution.py:121
  102.8 15.7 %collective-permute-done.5 = bf16[2,4,16384]{2,1,0:T(4,128)(2,1)S(1)} collective-permute-done((bf16[2,4,16384]{2,1,0:T(4,128)(2,1)S(1)}, bf16[2,4,16384]{2,1,0:T(4,128)(2,1)S(1)}, u32[]{:S(2)}, u32[]{:S(2)}) %collective-permute-start.5) | collective-permute-done | bytes 262176 | tf_op jit(solution)/shard_map/ppermute | solution.py:121
  120.6 10.7 %while.79 = (s32[]{:T(128)}, f32[256,256]{1,0:T(8,128)S(1)}, f32[256,6]{0,1:T(8,128)S(1)}, bf16[16,16384]{1,0:T(8,128)(2,1)S(1)}, bf16[16,16384]{1,0:T(8,128)(2,...) while((s32[]{:T(128)}, f32[256,256]{1,0:T(8,128)S(1)}, ...), condition=%wide.region_1.2_spmd.clone, body=%wide.region_0.1_spmd.clone.sunk | while | flops 551816192 | bytes 8204454 | solution.py:142
  134.9 9.7 %collective-permute-done.8 = f32[256,262]{1,0:T(8,128)S(1)} collective-permute-done((f32[256,262]{1,0:T(8,128)S(1)}, f32[256,262]{1,0:T(8,128)S(1)}, u32[]{:S(2)}, u32[]{:S(2)}) %collective-permute-start.8) | collective-permute-done | bytes 268320 | tf_op jit(solution)/shard_map/ppermute | solution.py:39
  145.5 9.5 %collective-permute-done.9 = f32[256,262]{1,0:T(8,128)S(1)} collective-permute-done((f32[256,262]{1,0:T(8,128)S(1)}, f32[256,262]{1,0:T(8,128)S(1)}, u32[]{:S(2)}, u32[]{:S(2)}) %collective-permute-start.9) | collective-permute-done | bytes 268320 | tf_op jit(solution)/shard_map/ppermute | solution.py:39
  155.0 2.9 %collective-permute-start.10 = (f32[256,262]{1,0:T(8,128)S(1)}, f32[256,262]{1,0:T(8,128)S(1)}, u32[]{:S(2)}, u32[]{:S(2)}) collective-permute-start(f32[256,262]{1,0:T(8,128)S(1)} %add.218), channel_id=1, source_target_pairs={{0,8},{4,12},{8,0},{12,4},{1,9},{5,13},{9,1},{13,5},{2,10},{6,14},... | collective-permute-start | bytes 804872 | tf_op jit(solution)/shard_map/ppermute | solution.py:39
  157.9 16.1 %collective-permute-done.10 = f32[256,262]{1,0:T(8,128)S(1)} collective-permute-done((f32[256,262]{1,0:T(8,128)S(1)}, f32[256,262]{1,0:T(8,128)S(1)}, u32[]{:S(2)}, u32[]{:S(2)}) %collective-permute-start.10) | collective-permute-done | bytes 268320 | tf_op jit(solution)/shard_map/ppermute | solution.py:39
  174.1 2.3 %gather_fusion = f32[256]{0:T(256)S(1)} fusion(f32[256,256]{1,0:T(8,128)S(1)} %slice.69, s32[256]{0:T(256)S(1)} %bitcast.78), kind=kCustom, calls=%fused_computation | custom fusion | bytes 4096 | tf_op jit(solution)/shard_map/jit(diagonal)/cond/branch_0_fun/gather | solution.py:151
  176.7 12.1 %while.77 = (s32[]{:T(128)}, f32[6,256]{1,0:T(8,128)S(1)}, f32[3,6,64]{2,1,0:T(8,128)}, s32[3,6,256]{2,1,0:T(8,128)}, f32[6,256]{1,0:T(8,128)S(1)}, /*index=5*/f...) while((s32[]{:T(128)}, f32[6,256]{1,0:T(8,128)S(1)}, f32[3,6,64]{2,1,0:T(8,128)}, ...), condition=%wide.region_8.9_spmd, body=%wide.region_2.8_spmd.sunk | while | flops 9474058 | bytes 660566 | solution.py:186
  177.9 2.2 %while.80 = (s32[]{:T(128)}, f32[6,256]{1,0:T(8,128)S(1)}, f32[6,256]{1,0:T(8,128)S(1)}, f32[6,256]{1,0:T(8,128)S(1)}, f32[6]{0:T(128)S(1)}, /*index=5*/f32[6,256]{1,0:T(8,128)S(1)}, f32[256,256]{1,0:T(8,128)S(1)}, s32[]{:T(128)}) while((s32[]{:T(128)}, f32[6,256]{1,0:T(8,128)S(1)}, f32[6,256]{1,0:T(8,128)S(1)}, f32[6,256]{1,0:T(8,128)S(1)}, ...), condition=%wide.region_7.7_spmd, body=%wide.region_4.6_spmd.sunk | while | flops 4740110 | bytes 330125 | solution.py:179
  188.9 6.4 %while.78 = (s32[]{:T(128)}, bf16[6,16384]{1,0:T(8,128)(2,1)S(1)}, bf16[6,16384]{1,0:T(8,128)(2,1)}, bf16[16,16384]{1,0:T(8,128)(2,1)S(1)}, bf16[16,16384]{1,0:T...) while((s32[]{:T(128)}, bf16[6,16384]{1,0:T(8,128)(2,1)S(1)}, ...), condition=%wide.region_10.11_spmd, body=%wide.region_9.10_spmd.sunk | while | flops 14884870 | bytes 5623963 | solution.py:207
  195.3 21.9 %all_gather.3 = bf16[6,65536]{1,0:T(8,128)(2,1)S(1)} all-gather(bf16[6,16384]{1,0:T(8,128)(2,1)S(1)} %get-tuple-element.439), channel_id=1, replica_groups=mesh['groups'=2,'cols'=4,'slab'=2,'rep'=2] {'cols'}, dimensions={1}, use_global_device_ids=true | all-gather | bytes 983040 | tf_op jit(solution)/shard_map/all_gather | solution.py:208
  (163 shorter events, 57.5 us)
Async XLA Ops:
  0.6 15.8 %copy-start.2 = (s32[4]{0:T(128)S(1)}, s32[4]{0:T(128)}, u32[]{:S(2)}) copy-start(s32[4]{0:T(128)} %param.14) | copy-start | bytes 52
  0.6 15.9 %copy-start.1 = (bf16[6,4,256,64]{2,3,1,0:T(8,128)(2,1)S(1)}, bf16[6,4,256,64]{2,3,1,0:T(8,128)(2,1)}, u32[]{:S(2)}) copy-start(bf16[6,4,256,64]{2,3,1,0:T(8,128)(2,1)} %param.13) | copy-start | bytes 2359300
  13.4 10.1 %collective-permute-start = (bf16[4,4,1024,5]{2,3,1,0:T(8,128)(2,1)S(1)}, bf16[4,4,1024,5]{2,3,1,0:T(8,128)(2,1)S(1)}, u32[]{:S(2)}, u32[]{:S(2)}) collective-permute-start(bf16[4,4,1024,5]{2,3,1,0:T(8,128)(2,1)S(1)} %get-tuple-element.563), channel_id=1, source_target_pairs={{0,2},{2,0},{1,3},{3,1},{4,6},{6,4},{5,7},{7,5},{8,10},{10,8},{9,1... | collective-permute-start | bytes 491528 | tf_op jit(solution)/shard_map/ppermute | solution.py:24
  16.4 11.9 %collective-permute-start.1 = (bf16[4,4,1024,5]{2,3,1,0:T(8,128)(2,1)S(1)}, bf16[4,4,1024,5]{2,3,1,0:T(8,128)(2,1)S(1)}, u32[]{:S(2)}, u32[]{:S(2)}) collective-permute-start(bf16[4,4,1024,5]{2,3,1,0:T(8,128)(2,1)S(1)} %get-tuple-element.564), channel_id=1, source_target_pairs={{2,0},{0,2},{3,1},{1,3},{6,4},{4,6},{7,5},{5,7},{10,8},{8,10},{11,... | collective-permute-start | bytes 491528 | tf_op jit(solution)/shard_map/ppermute | solution.py:25
  33.8 3.5 %copy-start = (bf16[4,4,1024,266]{2,3,1,0:T(8,128)(2,1)}, bf16[4,4,1024,266]{2,3,1,0:T(8,128)(2,1)S(1)}, u32[]{:S(2)}) copy-start(bf16[4,4,1024,266]{2,3,1,0:T(8,128)(2,1)S(1)} %pad_maximum_fusion) | copy-start | bytes 26148868
  38.5 4.6 %collective-permute-start.2 = (bf16[4,4,5,266]{3,1,2,0:T(4,128)(2,1)S(1)}, bf16[4,4,5,266]{3,1,2,0:T(4,128)(2,1)S(1)}, u32[]{:S(2)}, u32[]{:S(2)}) collective-permute-start(bf16[4,4,5,266]{3,1,2,0:T(4,128)(2,1)S(1)} %copy.27), channel_id=1, source_target_pairs={{0,1},{1,0},{2,3},{3,2},{4,5},{5,4},{6,7},{7,6},{8,9},{9,8},{10,11... | collective-permute-start | bytes 127688 | tf_op jit(solution)/shard_map/ppermute | solution.py:24
  39.1 4.6 %collective-permute-start.3 = (bf16[4,4,5,266]{3,1,2,0:T(4,128)(2,1)S(1)}, bf16[4,4,5,266]{3,1,2,0:T(4,128)(2,1)S(1)}, u32[]{:S(2)}, u32[]{:S(2)}) collective-permute-start(bf16[4,4,5,266]{3,1,2,0:T(4,128)(2,1)S(1)} %copy.28), channel_id=1, source_target_pairs={{1,0},{0,1},{3,2},{2,3},{5,4},{4,5},{7,6},{6,7},{9,8},{8,9},{11,10... | collective-permute-start | bytes 127688 | tf_op jit(solution)/shard_map/ppermute | solution.py:25
  92.2 10.7 %collective-permute-start.4 = (bf16[2,4,16384]{2,1,0:T(4,128)(2,1)S(1)}, bf16[2,4,16384]{2,1,0:T(4,128)(2,1)S(1)}, u32[]{:S(2)}, u32[]{:S(2)}) collective-permute-start(bf16[2,4,16384]{2,1,0:T(4,128)(2,1)S(1)} %get-tuple-element.570), channel_id=1, source_target_pairs={{0,12},{4,0},{8,4},{12,8},{1,13},{5,1},{9,5},{13,9},{2,14},{6,2},{... | collective-permute-start | bytes 786440 | tf_op jit(solution)/shard_map/ppermute | solution.py:121
  96.1 22.5 %collective-permute-start.5 = (bf16[2,4,16384]{2,1,0:T(4,128)(2,1)S(1)}, bf16[2,4,16384]{2,1,0:T(4,128)(2,1)S(1)}, u32[]{:S(2)}, u32[]{:S(2)}) collective-permute-start(bf16[2,4,16384]{2,1,0:T(4,128)(2,1)S(1)} %get-tuple-element.569), channel_id=1, source_target_pairs={{0,8},{4,12},{8,0},{12,4},{1,9},{5,13},{9,1},{13,5},{2,10},{6,14},... | collective-permute-start | bytes 786440 | tf_op jit(solution)/shard_map/ppermute | solution.py:121
  96.1 22.5 %collective-permute-start.6 = (bf16[2,4,16384]{2,1,0:T(4,128)(2,1)S(1)}, bf16[2,4,16384]{2,1,0:T(4,128)(2,1)S(1)}, u32[]{:S(2)}, u32[]{:S(2)}) collective-permute-start(bf16[2,4,16384]{2,1,0:T(4,128)(2,1)S(1)} %get-tuple-element.568), channel_id=1, source_target_pairs={{0,4},{4,8},{8,12},{12,0},{1,5},{5,9},{9,13},{13,1},{2,6},{6,10},{... | collective-permute-start | bytes 786440 | tf_op jit(solution)/shard_map/ppermute | solution.py:121
  131.5 1.8 collective-permute-start.7
  133.3 11.2 %collective-permute-start.8 = (f32[256,262]{1,0:T(8,128)S(1)}, f32[256,262]{1,0:T(8,128)S(1)}, u32[]{:S(2)}, u32[]{:S(2)}) collective-permute-start(f32[256,262]{1,0:T(8,128)S(1)} %fusion.184), channel_id=1, source_target_pairs={{0,2},{2,0},{1,3},{3,1},{4,6},{6,4},{5,7},{7,5},{8,10},{10,8},{9,1... | collective-permute-start | bytes 804872 | tf_op jit(solution)/shard_map/ppermute | solution.py:39
  144.6 10.4 %collective-permute-start.9 = (f32[256,262]{1,0:T(8,128)S(1)}, f32[256,262]{1,0:T(8,128)S(1)}, u32[]{:S(2)}, u32[]{:S(2)}) collective-permute-start(f32[256,262]{1,0:T(8,128)S(1)} %add.217), channel_id=1, source_target_pairs={{0,4},{4,0},{8,12},{12,8},{1,5},{5,1},{9,13},{13,9},{2,6},{6,2},{1... | collective-permute-start | bytes 804872 | tf_op jit(solution)/shard_map/ppermute | solution.py:39
  155.0 19.0 %collective-permute-start.10 = (f32[256,262]{1,0:T(8,128)S(1)}, f32[256,262]{1,0:T(8,128)S(1)}, u32[]{:S(2)}, u32[]{:S(2)}) collective-permute-start(f32[256,262]{1,0:T(8,128)S(1)} %add.218), channel_id=1, source_target_pairs={{0,8},{4,12},{8,0},{12,4},{1,9},{5,13},{9,1},{13,5},{2,10},{6,14},... | collective-permute-start | bytes 804872 | tf_op jit(solution)/shard_map/ppermute | solution.py:39
